TPU v7x, 128 devices: a whole 4x4x4 slice. The times are simulated.
128 devices in a mesh: dp: 4 (over z_lo, core), tensor: 32 (over y, x, z_hi).
Axes of the slice: x: 4, y: 4, z: 4 (z_hi: 2, z_lo: 2; z = z_hi * 2 + z_lo), core: 2. Of those that a mesh axis runs over, the one named last changes fastest.
Arguments:
- stream: bfloat16 [6144, 2560], P(('dp', 'tensor')), may hold values from -26 to 26
- lengths: int32 [4, 6], P('dp'), may hold values from 16 to 768, as said below
- page_table: int32 [384], P('dp'), may hold values from 0 to 383, as said below
- request_prompt: int32 [64], P('dp'), may hold values from 0 to 23
- attn_gain: bfloat16 [2560], replicated, may hold values from 0.099609375 to 1.8984375
- query_gain: bfloat16 [128], replicated, may hold values from 0.5 to 10, as said below
- key_gain: bfloat16 [128], replicated, may hold values from 0.5 to 10, as said below
- mlp_gain: bfloat16 [2560], replicated, may hold values from 0.099609375 to 1.8984375
- w_query: bfloat16 [2560, 4096], P(None, 'tensor'), may hold values from -0.125 to 0.125
- key_value_weight: bfloat16 [2560, 2048], P(None, 'tensor'), may hold values from -0.125 to 0.125
- w_out: bfloat16 [4096, 2560], P('tensor'), may hold values from -0.5 to 0.5
- w_gate: bfloat16 [2560, 9728], P(None, 'tensor'), may hold values from -0.125 to 0.125
- w_up: bfloat16 [2560, 9728], P(None, 'tensor'), may hold values from -0.125 to 0.125
- w_down: bfloat16 [9728, 2560], P('tensor'), may hold values from -0.0625 to 0.0625
Outputs:
- layer_out: bfloat16 [6144, 2560], P(('dp', 'tensor'))
- paged_key_value_cache: bfloat16 [384, 16, 2048], P('dp', None, 'tensor')
- request_state: bfloat16 [64, 2560], P('dp', 'tensor')
Inputs may be any that keep to these rules, and one draw needn't show every extreme that they name: Every length is a multiple of 16; each batch's lengths add up to 1536, and the largest length of each batch is exactly 768. page_table is a permutation of all global slots; slot v belongs to owner v // 96, and each batch writes exactly 24 pages to each owner. `query_gain`: positive gains. `key_gain`: positive gains.
All inputs are finite; a program needn't handle non-finite values.
Results may differ from a plain program's by a relative error of at most 0.02.
The roundings to bfloat16 on the way count: a program that leaves them out, or rounds other values in their place, can miss the bound.
Values may be sent and summed in bfloat16 or wider, within the bound.
No kernel may reach another device: no remote copies, remote signals or barrier semaphores. Data moves between devices by JAX's collectives and lax.ppermute only.
A program may use at most 128 MiB of HBM per device.

v0:
```python
import math
import jax
import jax.numpy as jnp
from jax import lax
from jax.sharding import PartitionSpec as P

KEY_VALUE_HEADS = 8
HEAD_SIZE = 128
PAGE_TOKENS = 16
TENSOR = ("ty", "tx", "tz")
TENSOR_SHAPE = (4, 4, 2)
epsilon = 1e-06
rope_base = 1000000.0


def partner_2(value, axis, bit):
    mask = 2**bit
    pairs = [(source, source ^ mask) for source in range(lax.axis_size(axis))]
    return lax.ppermute(value, axis, pairs)


def scatter_sum(partial, parts):
    pieces = partial.reshape((parts, partial.shape[0] // parts) + partial.shape[1:])
    got = lax.all_to_all(pieces, TENSOR, 0, 0, tiled=True)
    return jnp.sum(got.astype(jnp.float32), axis=0)


def gather_rows(rows):
    rows = lax.all_gather(rows, "tz", axis=0, tiled=True)
    return lax.all_gather(rows, ("ty", "tx"), axis=0, tiled=True)


def row_norm(inputs, gain):
    inputs = inputs.astype(jnp.float32)
    scale = lax.rsqrt(jnp.mean(inputs * inputs, axis=-1, keepdims=True) + epsilon)
    return inputs * scale * gain.astype(jnp.float32)


def rotate(inputs, position):
    half_dim = inputs.shape[-1] // 2
    frequency = rope_base ** (-2.0 * jnp.arange(half_dim, dtype=jnp.float32) / inputs.shape[-1])
    angles = position.astype(jnp.float32)[:, None] * frequency[None, :]
    cosine = jnp.cos(angles)[:, None, :]
    sine_part = jnp.sin(angles)[:, None, :]
    front = inputs[..., :half_dim]
    second = inputs[..., half_dim:]
    return jnp.concatenate(
        [front * cosine - second * sine_part, second * cosine + front * sine_part], axis=-1
    )


def prompt_layout(lengths_row, token_count):
    prompt_ends = jnp.cumsum(lengths_row)
    prompt_starts = prompt_ends - lengths_row
    row_ids = jnp.arange(token_count, dtype=jnp.int32)
    prompt = jnp.sum((row_ids[:, None] >= prompt_ends[None, :]).astype(jnp.int32), axis=1)
    inside = (row_ids[:, None] >= prompt_starts[None, :]) & (
        row_ids[:, None] < prompt_ends[None, :]
    )
    offset = jnp.sum(jnp.where(inside, prompt_starts[None, :], 0), axis=1)
    return (prompt, row_ids - offset, prompt_starts, prompt_ends)


def per_device(
    stream,
    lengths,
    page_table,
    request_prompt,
    attn_gain,
    query_gain,
    key_gain,
    mlp_gain,
    w_query,
    key_value_weight,
    w_out,
    w_gate,
    w_up,
    w_down,
):
    tok_dev = stream.shape[0]
    tensor_element_count = lax.axis_size(TENSOR)
    token_count = tok_dev * tensor_element_count
    my_index = lax.axis_index(TENSOR)
    heads_dev = w_query.shape[1] // HEAD_SIZE
    query_cols = heads_dev * HEAD_SIZE
    prompt, position, prompt_starts, prompt_ends = prompt_layout(lengths[0], token_count)
    portion = gather_rows(row_norm(stream, attn_gain).astype(jnp.bfloat16))
    key_value_group = tensor_element_count // KEY_VALUE_HEADS
    head_weight = key_value_weight
    for bit_id in range(key_value_group.bit_length() - 1):
        partner = partner_2(head_weight, TENSOR, bit_id)
        upper_half = my_index // 2**bit_id % 2
        head_weight = jnp.where(
            upper_half == 1,
            jnp.concatenate([partner, head_weight], axis=1),
            jnp.concatenate([head_weight, partner], axis=1),
        )
    joined = jnp.concatenate(
        [
            jnp.dot(portion, w_query, preferred_element_type=jnp.float32),
            jnp.dot(portion, head_weight, preferred_element_type=jnp.float32),
        ],
        axis=1,
    )
    queries = joined[:, :query_cols].reshape(token_count, heads_dev, HEAD_SIZE)
    kv_part = joined[:, query_cols:].astype(jnp.bfloat16)
    key_flat = rotate(row_norm(kv_part[:, None, :HEAD_SIZE], key_gain), position).astype(
        jnp.bfloat16
    )[:, 0, :]
    value_matrix_rows = kv_part[:, HEAD_SIZE:]
    q_rot = rotate(row_norm(queries, query_gain), position).astype(jnp.bfloat16)
    piece_cols = key_value_weight.shape[1]
    head_rows = jnp.concatenate([key_flat, value_matrix_rows], axis=1)
    own_cols = lax.dynamic_slice_in_dim(
        head_rows, my_index % key_value_group * piece_cols, piece_cols, 1
    )
    page_count = token_count // PAGE_TOKENS
    page_rows = own_cols.reshape(page_count, PAGE_TOKENS, piece_cols)
    group_count = lax.axis_size("dp")
    capacity = page_count // group_count
    owners = page_table // page_count
    slot_ids = page_table % page_count
    hits = (owners[:, None] == jnp.arange(group_count, dtype=jnp.int32)[None, :]).astype(jnp.int32)
    order_in = jnp.sum((jnp.cumsum(hits, axis=0) - hits) * hits, axis=1)
    buffer_pos = owners * capacity + order_in
    source = (
        jnp.zeros((page_count,), jnp.int32)
        .at[buffer_pos]
        .set(jnp.arange(page_count, dtype=jnp.int32))
    )
    send_pages = page_rows[source].reshape(group_count, capacity, PAGE_TOKENS, piece_cols)
    send_slots = slot_ids[source].reshape(group_count, capacity)
    got_pages, got_slots = (
        lax.all_to_all(send_pages, "dp", split_axis=0, concat_axis=0, tiled=True),
        lax.all_to_all(send_slots, "dp", split_axis=0, concat_axis=0, tiled=True),
    )
    paged_key_value_cache = (
        jnp.zeros((page_count, PAGE_TOKENS, piece_cols), jnp.bfloat16)
        .at[got_slots.reshape(-1)]
        .set(got_pages.reshape(page_count, PAGE_TOKENS, piece_cols))
    )
    block_rows = min(512, token_count)
    block_total = token_count // block_rows
    score_scale = math.sqrt(HEAD_SIZE)
    all_ids = jnp.arange(token_count, dtype=jnp.int32)
    local_ids = jnp.arange(block_rows, dtype=jnp.int32)

    def dense_block(block_index):
        first_row = block_index * block_rows
        q_block = lax.dynamic_slice_in_dim(q_rot, first_row, block_rows, 0)
        q_prompt = lax.dynamic_slice_in_dim(prompt, first_row, block_rows, 0)
        row_ids = first_row + local_ids
        scores = (
            jnp.einsum("qhd,kd->hqk", q_block, key_flat, preferred_element_type=jnp.float32)
            / score_scale
        )
        allowed = ((q_prompt[:, None] == prompt[None, :]) & (row_ids[:, None] >= all_ids[None, :]))[
            None
        ]
        peak = jnp.max(jnp.where(allowed, scores, -jnp.inf), axis=2, keepdims=True)
        weight = jnp.where(allowed, jnp.exp(scores - peak), 0.0)
        total_weight = jnp.sum(weight, axis=2, keepdims=True)
        running = jnp.einsum(
            "hqk,kd->hqd",
            weight.astype(jnp.bfloat16),
            value_matrix_rows,
            preferred_element_type=jnp.float32,
        )
        return (running / total_weight).astype(jnp.bfloat16)

    block_ids = jnp.arange(block_total, dtype=jnp.int32)
    blocks_out = lax.map(dense_block, block_ids)
    attn = jnp.transpose(blocks_out, (0, 2, 1, 3)).reshape(token_count, query_cols)
    attn_sum = scatter_sum(
        jnp.dot(attn, w_out, preferred_element_type=jnp.float32).astype(jnp.bfloat16),
        tensor_element_count,
    )
    resid = (stream.astype(jnp.float32) + attn_sum).astype(jnp.bfloat16)
    portion = gather_rows(row_norm(resid, mlp_gain).astype(jnp.bfloat16))
    paged_key_value_cache, portion = lax.optimization_barrier((paged_key_value_cache, portion))
    gate_rows = jnp.dot(portion, w_gate, preferred_element_type=jnp.float32)
    upward = jnp.dot(portion, w_up, preferred_element_type=jnp.float32)
    hidden = (jax.nn.silu(gate_rows) * upward).astype(jnp.bfloat16)
    mlp_sum = scatter_sum(
        jnp.dot(hidden, w_down, preferred_element_type=jnp.float32).astype(jnp.bfloat16),
        tensor_element_count,
    )
    layer_out = (resid.astype(jnp.float32) + mlp_sum).astype(jnp.bfloat16)
    width = w_down.shape[1]
    feat = width // tensor_element_count
    nprompt = prompt_ends.shape[0]
    end_pick = ((prompt_ends - 1)[:, None] == all_ids[None, :]).astype(jnp.bfloat16)
    end_hidden = jnp.dot(end_pick, hidden, preferred_element_type=jnp.float32).astype(jnp.bfloat16)
    end_down = jnp.dot(end_hidden, w_down, preferred_element_type=jnp.float32).astype(jnp.bfloat16)
    my_rows = my_index * tok_dev + jnp.arange(tok_dev, dtype=jnp.int32)
    select = ((prompt_ends - 1)[:, None] == my_rows[None, :]).astype(jnp.bfloat16)
    end_resid = jnp.dot(select, resid, preferred_element_type=jnp.float32)
    end_terms = jnp.stack([end_down.astype(jnp.float32), end_resid])
    end_blocks = jnp.transpose(
        end_terms.reshape(2, nprompt, tensor_element_count, feat), (2, 0, 1, 3)
    )
    end_sums = lax.psum_scatter(end_blocks, TENSOR, scatter_dimension=0, tiled=True)[0]
    end_rows = (end_sums[0] + end_sums[1]).astype(jnp.bfloat16)
    table = lax.all_gather(end_rows, "dp", axis=0, tiled=True)
    pick = (request_prompt[:, None] == jnp.arange(table.shape[0], dtype=jnp.int32)[None, :]).astype(
        jnp.bfloat16
    )
    request_state = jnp.dot(pick, table, preferred_element_type=jnp.float32).astype(jnp.bfloat16)
    return (layer_out, paged_key_value_cache, request_state)


def solution(mesh):
    placed = (
        P(("dp",) + TENSOR, None),
        P("dp", None),
        P("dp"),
        P("dp"),
        P(),
        P(),
        P(),
        P(),
        P(None, TENSOR),
        P(None, TENSOR),
        P(TENSOR, None),
        P(None, TENSOR),
        P(None, TENSOR),
        P(TENSOR, None),
    )
    dp_size = mesh.shape["dp"]
    fine = jax.sharding.Mesh(mesh.devices.reshape((dp_size,) + TENSOR_SHAPE), ("dp",) + TENSOR)
    return jax.shard_map(
        per_device,
        mesh=fine,
        in_specs=placed,
        out_specs=(P(("dp",) + TENSOR, None), P("dp", None, TENSOR), P("dp", TENSOR)),
        check_vma=False,
    )
```

profile of v0, /device:TPU:1, one launch (start us, length us, event | category | flops | bytes accessed | tf_op | source)
XLA Modules:
  0.0 795.8 jit_solution(10298598283091658743)
XLA Ops:
  7.2 1.2 fusion.46
  9.2 1.1 fusion.48
  10.2 10.8 %all_gather.15 = bf16[96,2560]{1,0:T(8,128)(2,1)} all-gather(bf16[48,2560]{1,0:T(8,128)(2,1)S(1)} %fusion.48), channel_id=1, replica_groups=mesh['dp'=4,'ty'=4,'tx'=4,'tz'=2] {'tz'}, dimensions={0}, use_global_device_ids=true | all-gather | bytes 737280 | tf_op jit(solution)/shard_map/all_gather | solution.py:29
  21.1 2.8 collective-permute-start
  24.7 1.2 convert_element_type.111
  25.9 1.2 convert_element_type.115
  27.1 3.8 collective-permute-done
  30.9 1.2 maximum_select_fusion.2
  32.1 1.3 collective-permute-start.1
  34.1 20.9 %collective-permute-done.1 = bf16[2560,128]{0,1:T(8,128)(2,1)} collective-permute-done((bf16[2560,128]{0,1:T(8,128)(2,1)S(1)}, bf16[2560,128]{0,1:T(8,128)(2,1)}, u32[]{:S(2)}, u32[]{:S(2)}) %collective-permute-start.1) | collective-permute-done | bytes 655392 | tf_op jit(solution)/shard_map/ppermute | solution.py:19
  54.9 41.6 %all-gather.4.cloned.1.call-done = bf16[1536,2560]{1,0:T(8,128)(2,1)} async-done(((bf16[96,2560]{1,0:T(8,128)(2,1)}), bf16[1536,2560]{1,0:T(8,128)(2,1)}) %all-gather.4.cloned.1.call-update) | async-done | bytes 7864336 | tf_op jit(solution)/shard_map/all_gather | solution.py:30
  96.5 5.9 convolution_convert_fusion.3
  102.6 3.8 multiply_reduce_fusion
  109.0 2.4 fusion.55
  111.4 0.9 copy.44
  113.1 18.2 %while.11 = (s32[]{:T(128)}, bf16[3,1,512,128]{3,2,1,0:T(8,128)(2,1)S(1)}, s32[3]{0:T(128)S(1)}, s32[1536]{0:T(1024)S(1)}, bf16[1536,1,128]{0,2,1:T(8,128)(2,1)}...) while((s32[]{:T(128)}, ...), condition=%wide.region_9.10_spmd.clone, body=%wide.region_6.9_spmd.clone.sunk | while | flops 416939520 | bytes 12107995 | solution.py:172
  114.4 2.2 select_reduce_fusion.4
  116.6 1.1 fusion.109
  117.7 1.5 fusion.110
  120.5 2.2 select_reduce_fusion.4
  122.7 1.1 fusion.109
  123.8 1.5 fusion.110
  126.6 2.2 select_reduce_fusion.4
  128.8 1.1 fusion.109
  129.9 1.5 fusion.110
  131.4 5.3 convolution_convert_fusion.1
  136.7 8.1 %all-to-all-start = ((bf16[32,48,2560]{2,1,0:T(8,128)(2,1)}), bf16[32,48,2560]{2,1,0:T(8,128)(2,1)}, u32[]{:S(2)}, u32[]{:S(2)}) async-start(bf16[32,48,2560]{2,1,0:T(8,128)(2,1)} %bitcast.96), calls=%async_computation | async-start | bytes 15728640 | tf_op jit(solution)/shard_map/all_to_all | solution.py:24
  145.1 115.4 %all-to-all-done = bf16[32,48,2560]{2,1,0:T(8,128)(2,1)} async-done(((bf16[32,48,2560]{2,1,0:T(8,128)(2,1)}), bf16[32,48,2560]{2,1,0:T(8,128)(2,1)}, u32[]{:S(2)}, u32[]{:S(2)}) %all-to-all-start) | async-done | bytes 7864352 | tf_op jit(solution)/shard_map/all_to_all | solution.py:24
  260.4 4.5 convert_reduce_fusion.1
  265.3 7.8 all_gather.17
  274.6 1.2 gather_fusion
  276.4 6.0 all-to-all-start.1
  282.4 3.0 all-to-all-done.1
  287.8 1.0 reshape.459
  288.8 4.0 all-to-all-start.2
  292.8 4.5 all-to-all-done.2
  297.6 3.5 scatter_fusion
  301.1 47.3 %all-gather.6.cloned.1.call-done = bf16[1536,2560]{1,0:T(8,128)(2,1)} async-done(((bf16[96,2560]{1,0:T(8,128)(2,1)}), bf16[1536,2560]{1,0:T(8,128)(2,1)}) %all-gather.6.cloned.1.call-update) | async-done | bytes 7864336 | tf_op jit(solution)/shard_map/all_gather | solution.py:30
  348.4 5.6 fusion.84
  354.7 2.7 fusion.28
  357.4 6.5 convolution_convert_fusion
  363.9 8.1 %all-to-all-start.3 = ((bf16[32,48,2560]{2,1,0:T(8,128)(2,1)}), bf16[32,48,2560]{2,1,0:T(8,128)(2,1)}, u32[]{:S(2)}, u32[]{:S(2)}) async-start(bf16[32,48,2560]{2,1,0:T(8,128)(2,1)} %bitcast.97), calls=%async_computation.3 | async-start | bytes 15728640 | tf_op jit(solution)/shard_map/all_to_all | solution.py:24
  372.4 1.0 fusion.27
  375.1 1.1 copy.50
  376.1 380.2 %all-reduce.3.cloned.1.call-done = f32[32,2,6,80]{3,1,0,2:T(2,128)} async-done(((f32[32,2,6,80]{3,1,0,2:T(2,128)}), f32[32,2,6,80]{3,1,0,2:T(2,128)}) %all-reduce.3.cloned.1.call-update) | async-done | bytes 122896
  756.3 1.4 fusion.75
  757.8 25.4 %all-gather = bf16[1,1,24,80]{3,1,0,2:T(2,128)(2,1)S(1)} all-gather(bf16[1,1,6,80]{3,1,0,2:T(2,128)(2,1)S(1)} %fusion.75), channel_id=2, replica_groups=mesh['dp'=4,'ty'=4,'tx'=4,'tz'=2] {'dp'}, dimensions={2}, use_global_device_ids=true | all-gather | bytes 4800 | tf_op jit(solution)/shard_map/all_gather | solution.py:204
  783.9 4.5 convert_reduce_fusion
  (100 shorter events, 17.2 us)
Async XLA Ops:
  7.2 350.2 %copy-start = (bf16[304,2560]{1,0:T(8,128)(2,1)S(1)}, bf16[304,2560]{1,0:T(8,128)(2,1)}, u32[]{:S(2)}) copy-start(bf16[304,2560]{1,0:T(8,128)(2,1)} %param.29) | copy-start | bytes 4669444
  7.2 26.8 %copy-start.11 = (s32[1,6]{1,0:T(1,128)S(1)}, s32[1,6]{1,0:T(1,128)}, u32[]{:S(2)}) copy-start(s32[1,6]{1,0:T(1,128)} %param.17) | copy-start | bytes 76
  7.2 89.3 %all-gather.4.cloned.1.call-start = ((), (), s32[]{:S(2)}) async-start(), calls=%async_computation.4 | async-start | bytes 8355840 | tf_op jit(solution)/shard_map/all_gather | solution.py:30
  21.1 9.8 %collective-permute-start = (bf16[2560,64]{0,1:T(8,128)(2,1)}, bf16[2560,64]{0,1:T(8,128)(2,1)S(1)}, u32[]{:S(2)}, u32[]{:S(2)}) collective-permute-start(bf16[2560,64]{0,1:T(8,128)(2,1)} %param.25), channel_id=1, source_target_pairs={{0,1},{1,0},{2,3},{3,2},{4,5},{5,4},{6,7},{7,6},{8,9},{9,8},{10,11... | collective-permute-start | bytes 983048 | tf_op jit(solution)/shard_map/ppermute | solution.py:19
  24.7 77.7 %copy-start.7 = (s32[6,1]{0,1:T(1,128)}, s32[6,1]{0,1:T(1,128)S(1)}, u32[]{:S(2)}) copy-start(s32[6,1]{0,1:T(1,128)S(1)} %reduce-window.4) | copy-start | bytes 76
  32.1 22.8 %collective-permute-start.1 = (bf16[2560,128]{0,1:T(8,128)(2,1)S(1)}, bf16[2560,128]{0,1:T(8,128)(2,1)}, u32[]{:S(2)}, u32[]{:S(2)}) collective-permute-start(bf16[2560,128]{0,1:T(8,128)(2,1)S(1)} %maximum_select_fusion.2), channel_id=1, source_target_pairs={{0,2},{1,3},{2,0},{3,1},{4,6},{5,7},{6,4},{7,5},{8,10},{9,11},{10,... | collective-permute-start | bytes 1966088 | tf_op jit(solution)/shard_map/ppermute | solution.py:19
  96.5 6.0 copy-start.1
  108.1 5.0 copy-start.3
  113.1 18.2 %copy-start.4 = (bf16[128,2560]{1,0:T(8,128)(2,1)S(1)}, bf16[128,2560]{1,0:T(8,128)(2,1)}, u32[]{:S(2)}) copy-start(bf16[128,2560]{1,0:T(8,128)(2,1)} %param.26) | copy-start | bytes 1966084
  114.4 3.2 copy-start.5
  120.5 3.2 copy-start.5
  126.6 3.2 copy-start.5
  136.7 8.3 %copy-start.6 = (bf16[2560]{0:T(1024)(128)(2,1)S(1)}, bf16[2560]{0:T(1024)(128)(2,1)}, u32[]{:S(2)}) copy-start(bf16[2560]{0:T(1024)(128)(2,1)} %param.23) | copy-start | bytes 15364
  136.7 123.7 %all-to-all-start = ((bf16[32,48,2560]{2,1,0:T(8,128)(2,1)}), bf16[32,48,2560]{2,1,0:T(8,128)(2,1)}, u32[]{:S(2)}, u32[]{:S(2)}) async-start(bf16[32,48,2560]{2,1,0:T(8,128)(2,1)} %bitcast.96), calls=%async_computation | async-start | bytes 15728640 | tf_op jit(solution)/shard_map/all_to_all | solution.py:24
  144.8 203.5 %all-gather.6.cloned.1.call-start = ((), (), s32[]{:S(2)}) async-start(), calls=%async_computation.5 | async-start | bytes 8355840 | tf_op jit(solution)/shard_map/all_gather | solution.py:30
  145.1 119.9 %copy-start.2 = (bf16[48,2560]{1,0:T(8,128)(2,1)S(1)}, bf16[48,2560]{1,0:T(8,128)(2,1)}, u32[]{:S(2)}) copy-start(bf16[48,2560]{1,0:T(8,128)(2,1)} %param.16) | copy-start | bytes 737284
  145.1 128.1 %copy-start.12 = (s32[96]{0:T(128)S(1)}, s32[96]{0:T(128)}, u32[]{:S(2)}) copy-start(s32[96]{0:T(128)} %param.18) | copy-start | bytes 1156
  276.4 9.0 %all-to-all-start.1 = ((s32[4,1,24]{2,1,0:T(1,128)}), s32[4,1,24]{2,1,0:T(1,128)S(1)}, u32[]{:S(2)}, u32[]{:S(2)}) async-start(s32[4,1,24]{2,1,0:T(1,128)} %bitcast.10), calls=%async_computation.1 | async-start | bytes 4096 | tf_op jit(solution)/shard_map/all_to_all | solution.py:135
  288.8 8.5 %all-to-all-start.2 = ((bf16[4,2,12288]{2,1,0:T(2,128)(2,1)}), bf16[4,2,12288]{2,1,0:T(2,128)(2,1)S(1)}, u32[]{:S(2)}, u32[]{:S(2)}) async-start(bf16[4,2,12288]{2,1,0:T(2,128)(2,1)} %reshape.459), calls=%async_computation.2 | async-start | bytes 393216 | tf_op jit(solution)/shard_map/all_to_all | solution.py:134
  348.3 6.0 copy-start.9
  348.4 6.4 copy-start.10
  363.9 8.2 %copy-start.8 = (s32[6,1]{0,1:T(1,128)S(1)}, s32[6,1]{0,1:T(1,128)}, u32[]{:S(2)}) copy-start(s32[6,1]{0,1:T(1,128)} %copy-done.7) | copy-start | bytes 76
  363.9 420.0 %all-to-all-start.3 = ((bf16[32,48,2560]{2,1,0:T(8,128)(2,1)}), bf16[32,48,2560]{2,1,0:T(8,128)(2,1)}, u32[]{:S(2)}, u32[]{:S(2)}) async-start(bf16[32,48,2560]{2,1,0:T(8,128)(2,1)} %bitcast.97), calls=%async_computation.3 | async-start | bytes 15728640 | tf_op jit(solution)/shard_map/all_to_all | solution.py:24
  372.0 2.4 copy-start.14
  372.0 411.1 %copy-start.13 = (s32[16]{0:T(128)S(1)}, s32[16]{0:T(128)}, u32[]{:S(2)}) copy-start(s32[16]{0:T(128)} %param.19) | copy-start | bytes 196
  372.0 384.3 %all-reduce.3.cloned.1.call-start = ((), (), s32[]{:S(2)}) async-start(), calls=%async_computation.6 | async-start | bytes 393216
Sparse Core Ops, SparseCore 0:
  21.2 75.2 all-gather.3
  273.3 74.9 all-gather.5
  375.9 380.3 all-reduce.2
where the time goes:
time: 797 us; the launch traced here: 796 us
  waiting for transfers between devices  617 us (77%)
  blocking collectives  44.1 us (6%)
  matrix products  42.8 us (5%)
  starting transfers between devices  30.6 us (4%)
  other arithmetic  29.9 us (4%)
  local copies, waits for them, and re-layouts  15.6 us (2%)
  between operations  14.2 us (2%)
    unnamed x4, waiting for transfers between devices  380 us
    all_to_all x2, waiting for transfers between devices, scatter_sum(): got = lax.all_to_all(pieces, TENSOR, 0, 0, tiled=True)  115 us
    all_gather x2, waiting for transfers between devices, gather_rows(): return lax.all_gather(rows, ('ty', 'tx'), axis=0, tiled=True)  88.8 us
    all_gather x1, blocking collectives, per_device(): table = lax.all_gather(end_rows, 'dp', axis=0, tiled=True)  25.4 us
    ppermute x2, waiting for transfers between devices, partner_2(): return lax.ppermute(value, axis, pairs)  24.7 us
    all_gather x2, blocking collectives, gather_rows(): rows = lax.all_gather(rows, 'tz', axis=0, tiled=True)  18.7 us
    all_to_all x2, starting transfers between devices, scatter_sum(): got = lax.all_to_all(pieces, TENSOR, 0, 0, tiled=True)  16.2 us
  transfers between devices with their start and end apart: 9, of which 8 were waited for; matrix products, arithmetic and copies ran while one was open for 3% of the time, Pallas kernels for 0%

commit v1 on v0

--- a/solution.py
+++ b/solution.py
@@ -201,7 +201,9 @@
     )
     end_sums = lax.psum_scatter(end_blocks, TENSOR, scatter_dimension=0, tiled=True)[0]
     end_rows = (end_sums[0] + end_sums[1]).astype(jnp.bfloat16)
-    table = lax.all_gather(end_rows, "dp", axis=0, tiled=True)
+    table = jnp.concatenate(
+        lax.all_to_all(jnp.stack([end_rows] * lax.axis_size("dp")), "dp", 0, 0), axis=0
+    )
     pick = (request_prompt[:, None] == jnp.arange(table.shape[0], dtype=jnp.int32)[None, :]).astype(
         jnp.bfloat16
     )

time: 797 us -> 701 us (0.88)
  waiting for transfers between devices: 617 us -> 514 us
  starting transfers between devices: 30.6 us -> 57 us
  blocking collectives: 44.1 us -> 18.7 us
    unnamed x4 -> x3, waiting for transfers between devices: 380 us -> 0.05 us
    reduce_scatter x0 -> x1, waiting for transfers between devices: none -> 160 us  [per_device(): lax.psum_scatter(end_blocks, TENSOR, scatter_dimension=0, tiled=True)[0]]
    all_to_all x2, waiting for transfers between devices: 115 us -> 233 us  [scatter_sum(): got = lax.all_to_all(pieces, TENSOR, 0, 0, tiled=True)]
    all_to_all x0 -> x1, starting transfers between devices: none -> 29.6 us  [per_device(): lax.all_to_all(jnp.stack([end_rows] * lax.axis_size('dp')), 'dp', 0, 0)]
    all_gather x1 -> x0, blocking collectives: 25.4 us -> none  [per_device(): table = lax.all_gather(end_rows, 'dp', axis=0, tiled=True)]
  transfers between devices with their start and end apart: 9 -> 10, of which waited for: 8 -> 9; matrix products, arithmetic and copies ran while one was open for 3% -> 3% of each run, Pallas kernels for 0% -> 0%
where the time goes in v1:
time: 701 us; the launch traced here: 693 us
  waiting for transfers between devices  514 us (73%)
  starting transfers between devices  57 us (8%)
  matrix products  42.7 us (6%)
  other arithmetic  29 us (4%)
  blocking collectives  18.7 us (3%)
  local copies, waits for them, and re-layouts  15.9 us (2%)
  between operations  14.2 us (2%)
    all_to_all x2, waiting for transfers between devices, scatter_sum(): got = lax.all_to_all(pieces, TENSOR, 0, 0, tiled=True)  233 us
    reduce_scatter x1, waiting for transfers between devices, per_device(): lax.psum_scatter(end_blocks, TENSOR, scatter_dimension=0, tiled=True)[0]  160 us
    all_gather x2, waiting for transfers between devices, gather_rows(): return lax.all_gather(rows, ('ty', 'tx'), axis=0, tiled=True)  88.5 us
    all_to_all x1, starting transfers between devices, per_device(): lax.all_to_all(jnp.stack([end_rows] * lax.axis_size('dp')), 'dp', 0, 0)  29.6 us
    ppermute x2, waiting for transfers between devices, partner_2(): return lax.ppermute(value, axis, pairs)  24.7 us
    all_gather x2, blocking collectives, gather_rows(): rows = lax.all_gather(rows, 'tz', axis=0, tiled=True)  18.7 us
  transfers between devices with their start and end apart: 10, of which 9 were waited for; matrix products, arithmetic and copies ran while one was open for 3% of the time, Pallas kernels for 0%

profile of v1, /device:TPU:1, one launch (start us, length us, event | category | flops | bytes accessed | tf_op | source)
XLA Modules:
  0.0 693.3 jit_solution(16706069264874183073)
XLA Ops:
  7.2 1.2 fusion.46
  9.2 1.1 fusion.48
  10.2 10.8 %all_gather.12 = bf16[96,2560]{1,0:T(8,128)(2,1)} all-gather(bf16[48,2560]{1,0:T(8,128)(2,1)S(1)} %fusion.48), channel_id=1, replica_groups=mesh['dp'=4,'ty'=4,'tx'=4,'tz'=2] {'tz'}, dimensions={0}, use_global_device_ids=true | all-gather | bytes 737280 | tf_op jit(solution)/shard_map/all_gather | solution.py:29
  21.1 2.8 collective-permute-start
  24.7 1.2 convert_element_type.113
  25.9 1.2 convert_element_type.117
  27.1 3.8 collective-permute-done
  30.9 1.2 maximum_select_fusion.2
  32.1 1.3 collective-permute-start.1
  34.1 20.9 %collective-permute-done.1 = bf16[2560,128]{0,1:T(8,128)(2,1)} collective-permute-done((bf16[2560,128]{0,1:T(8,128)(2,1)S(1)}, bf16[2560,128]{0,1:T(8,128)(2,1)}, u32[]{:S(2)}, u32[]{:S(2)}) %collective-permute-start.1) | collective-permute-done | bytes 655392 | tf_op jit(solution)/shard_map/ppermute | solution.py:19
  54.9 41.6 %all-gather.3.cloned.1.call-done = bf16[1536,2560]{1,0:T(8,128)(2,1)} async-done(((bf16[96,2560]{1,0:T(8,128)(2,1)}), bf16[1536,2560]{1,0:T(8,128)(2,1)}) %all-gather.3.cloned.1.call-update) | async-done | bytes 7864336 | tf_op jit(solution)/shard_map/all_gather | solution.py:30
  96.5 5.9 convolution_convert_fusion.3
  102.6 3.8 multiply_reduce_fusion
  109.0 2.4 fusion.55
  111.4 0.9 copy.36
  113.1 18.2 %while.11 = (s32[]{:T(128)}, bf16[3,1,512,128]{3,2,1,0:T(8,128)(2,1)S(1)}, s32[3]{0:T(128)S(1)}, s32[1536]{0:T(1024)S(1)}, bf16[1536,1,128]{0,2,1:T(8,128)(2,1)}...) while((s32[]{:T(128)}, ...), condition=%wide.region_9.10_spmd.clone, body=%wide.region_6.9_spmd.clone.sunk | while | flops 416939520 | bytes 12107995 | solution.py:172
  114.4 2.2 select_reduce_fusion.4
  116.6 1.1 fusion.109
  117.7 1.5 fusion.110
  120.5 2.2 select_reduce_fusion.4
  122.7 1.1 fusion.109
  123.8 1.5 fusion.110
  126.6 2.2 select_reduce_fusion.4
  128.8 1.1 fusion.109
  129.9 1.5 fusion.110
  131.4 5.3 convolution_convert_fusion.1
  136.7 8.1 %all-to-all-start = ((bf16[32,48,2560]{2,1,0:T(8,128)(2,1)}), bf16[32,48,2560]{2,1,0:T(8,128)(2,1)}, u32[]{:S(2)}, u32[]{:S(2)}) async-start(bf16[32,48,2560]{2,1,0:T(8,128)(2,1)} %bitcast.89), calls=%async_computation | async-start | bytes 15728640 | tf_op jit(solution)/shard_map/all_to_all | solution.py:24
  145.1 115.3 %all-to-all-done = bf16[32,48,2560]{2,1,0:T(8,128)(2,1)} async-done(((bf16[32,48,2560]{2,1,0:T(8,128)(2,1)}), bf16[32,48,2560]{2,1,0:T(8,128)(2,1)}, u32[]{:S(2)}, u32[]{:S(2)}) %all-to-all-start) | async-done | bytes 7864352 | tf_op jit(solution)/shard_map/all_to_all | solution.py:24
  260.4 4.5 convert_reduce_fusion.1
  265.3 7.9 %all_gather.14 = bf16[96,2560]{1,0:T(8,128)(2,1)} all-gather(bf16[48,2560]{1,0:T(8,128)(2,1)S(1)} %fusion.52), channel_id=1, replica_groups=mesh['dp'=4,'ty'=4,'tx'=4,'tz'=2] {'tz'}, dimensions={0}, use_global_device_ids=true | all-gather | bytes 737280 | tf_op jit(solution)/shard_map/all_gather | solution.py:29
  274.5 1.2 gather_fusion
  276.4 6.0 all-to-all-start.1
  282.4 3.0 all-to-all-done.1
  287.7 1.0 reshape.464
  288.7 4.0 all-to-all-start.2
  292.8 4.5 all-to-all-done.2
  297.6 3.5 scatter_fusion
  301.5 46.9 %all-gather.5.cloned.1.call-done = bf16[1536,2560]{1,0:T(8,128)(2,1)} async-done(((bf16[96,2560]{1,0:T(8,128)(2,1)}), bf16[1536,2560]{1,0:T(8,128)(2,1)}) %all-gather.5.cloned.1.call-update) | async-done | bytes 7864336 | tf_op jit(solution)/shard_map/all_gather | solution.py:30
  348.4 5.6 fusion.83
  354.8 2.7 fusion.28
  357.4 1.0 fusion.27
  359.4 159.9 %reduce-scatter.2.cloned.1.call-done = f32[1,2,6,80]{3,2,1,0:T(8,128)} async-done(((f32[32,2,6,80]{3,2,1,0:T(8,128)}), f32[1,2,6,80]{3,2,1,0:T(8,128)}) %reduce-scatter.2.cloned.1.call-update) | async-done | bytes 3856 | tf_op jit(solution)/shard_map/reduce_scatter | solution.py:202
  520.6 29.6 %all-to-all-start.4 = ((bf16[4,2,240]{2,1,0:T(2,128)(2,1)}), bf16[4,2,240]{2,1,0:T(2,128)(2,1)S(1)}, u32[]{:S(2)}, u32[]{:S(2)}) async-start(bf16[4,2,240]{2,1,0:T(2,128)(2,1)} %reshape.466), calls=%async_computation.5 | async-start | bytes 8192 | tf_op jit(solution)/shard_map/all_to_all | solution.py:205
  550.2 6.5 convolution_convert_fusion
  556.6 5.1 all-to-all-start.3
  561.7 1.1 copy.42
  563.7 117.9 %all-to-all-done.3 = bf16[32,48,2560]{2,1,0:T(8,128)(2,1)} async-done(((bf16[32,48,2560]{2,1,0:T(8,128)(2,1)}), bf16[32,48,2560]{2,1,0:T(8,128)(2,1)}, u32[]{:S(2)}, u32[]{:S(2)}) %all-to-all-start.3) | async-done | bytes 7864352 | tf_op jit(solution)/shard_map/all_to_all | solution.py:24
  681.5 4.5 convert_reduce_fusion
  (104 shorter events, 18.0 us)
Async XLA Ops:
  7.2 350.3 %copy-start = (bf16[304,2560]{1,0:T(8,128)(2,1)S(1)}, bf16[304,2560]{1,0:T(8,128)(2,1)}, u32[]{:S(2)}) copy-start(bf16[304,2560]{1,0:T(8,128)(2,1)} %param.29) | copy-start | bytes 4669444
  7.2 26.7 %copy-start.11 = (s32[1,6]{1,0:T(1,128)S(1)}, s32[1,6]{1,0:T(1,128)}, u32[]{:S(2)}) copy-start(s32[1,6]{1,0:T(1,128)} %param.17) | copy-start | bytes 76
  7.2 89.3 %all-gather.3.cloned.1.call-start = ((), (), s32[]{:S(2)}) async-start(), calls=%async_computation.6 | async-start | bytes 8355840 | tf_op jit(solution)/shard_map/all_gather | solution.py:30
  21.1 9.8 %collective-permute-start = (bf16[2560,64]{0,1:T(8,128)(2,1)}, bf16[2560,64]{0,1:T(8,128)(2,1)S(1)}, u32[]{:S(2)}, u32[]{:S(2)}) collective-permute-start(bf16[2560,64]{0,1:T(8,128)(2,1)} %param.25), channel_id=1, source_target_pairs={{0,1},{1,0},{2,3},{3,2},{4,5},{5,4},{6,7},{7,6},{8,9},{9,8},{10,11... | collective-permute-start | bytes 983048 | tf_op jit(solution)/shard_map/ppermute | solution.py:19
  24.7 77.7 %copy-start.7 = (s32[6,1]{0,1:T(1,128)}, s32[6,1]{0,1:T(1,128)S(1)}, u32[]{:S(2)}) copy-start(s32[6,1]{0,1:T(1,128)S(1)} %reduce-window.4) | copy-start | bytes 76
  32.1 22.8 %collective-permute-start.1 = (bf16[2560,128]{0,1:T(8,128)(2,1)S(1)}, bf16[2560,128]{0,1:T(8,128)(2,1)}, u32[]{:S(2)}, u32[]{:S(2)}) collective-permute-start(bf16[2560,128]{0,1:T(8,128)(2,1)S(1)} %maximum_select_fusion.2), channel_id=1, source_target_pairs={{0,2},{1,3},{2,0},{3,1},{4,6},{5,7},{6,4},{7,5},{8,10},{9,11},{10,... | collective-permute-start | bytes 1966088 | tf_op jit(solution)/shard_map/ppermute | solution.py:19
  96.5 6.0 copy-start.1
  108.1 5.0 copy-start.3
  113.1 18.2 %copy-start.4 = (bf16[128,2560]{1,0:T(8,128)(2,1)S(1)}, bf16[128,2560]{1,0:T(8,128)(2,1)}, u32[]{:S(2)}) copy-start(bf16[128,2560]{1,0:T(8,128)(2,1)} %param.26) | copy-start | bytes 1966084
  114.4 3.2 copy-start.5
  120.5 3.2 copy-start.5
  126.6 3.2 copy-start.5
  136.7 8.3 %copy-start.6 = (bf16[2560]{0:T(1024)(128)(2,1)S(1)}, bf16[2560]{0:T(1024)(128)(2,1)}, u32[]{:S(2)}) copy-start(bf16[2560]{0:T(1024)(128)(2,1)} %param.23) | copy-start | bytes 15364
  136.7 123.7 %all-to-all-start = ((bf16[32,48,2560]{2,1,0:T(8,128)(2,1)}), bf16[32,48,2560]{2,1,0:T(8,128)(2,1)}, u32[]{:S(2)}, u32[]{:S(2)}) async-start(bf16[32,48,2560]{2,1,0:T(8,128)(2,1)} %bitcast.89), calls=%async_computation | async-start | bytes 15728640 | tf_op jit(solution)/shard_map/all_to_all | solution.py:24
  144.8 203.6 %all-gather.5.cloned.1.call-start = ((), (), s32[]{:S(2)}) async-start(), calls=%async_computation.7 | async-start | bytes 8355840 | tf_op jit(solution)/shard_map/all_gather | solution.py:30
  145.1 119.9 %copy-start.2 = (bf16[48,2560]{1,0:T(8,128)(2,1)S(1)}, bf16[48,2560]{1,0:T(8,128)(2,1)}, u32[]{:S(2)}) copy-start(bf16[48,2560]{1,0:T(8,128)(2,1)} %param.16) | copy-start | bytes 737284
  145.1 128.1 %copy-start.12 = (s32[96]{0:T(128)S(1)}, s32[96]{0:T(128)}, u32[]{:S(2)}) copy-start(s32[96]{0:T(128)} %param.18) | copy-start | bytes 1156
  265.0 17.5 %copy-start.8 = (s32[6,1]{0,1:T(1,128)S(1)}, s32[6,1]{0,1:T(1,128)}, u32[]{:S(2)}) copy-start(s32[6,1]{0,1:T(1,128)} %copy-done.7) | copy-start | bytes 76
  276.4 9.0 %all-to-all-start.1 = ((s32[4,1,24]{2,1,0:T(1,128)}), s32[4,1,24]{2,1,0:T(1,128)S(1)}, u32[]{:S(2)}, u32[]{:S(2)}) async-start(s32[4,1,24]{2,1,0:T(1,128)} %bitcast.10), calls=%async_computation.1 | async-start | bytes 4096 | tf_op jit(solution)/shard_map/all_to_all | solution.py:135
  288.7 8.5 %all-to-all-start.2 = ((bf16[4,2,12288]{2,1,0:T(2,128)(2,1)}), bf16[4,2,12288]{2,1,0:T(2,128)(2,1)S(1)}, u32[]{:S(2)}, u32[]{:S(2)}) async-start(bf16[4,2,12288]{2,1,0:T(2,128)(2,1)} %reshape.464), calls=%async_computation.2 | async-start | bytes 393216 | tf_op jit(solution)/shard_map/all_to_all | solution.py:134
  292.8 226.4 %reduce-scatter.2.cloned.1.call-start = ((), (), s32[]{:S(2)}) async-start(), calls=%async_computation.8 | async-start | bytes 270336 | tf_op jit(solution)/shard_map/reduce_scatter | solution.py:202
  348.4 6.0 copy-start.9
  348.4 6.4 copy-start.10
  520.6 36.0 %all-to-all-start.4 = ((bf16[4,2,240]{2,1,0:T(2,128)(2,1)}), bf16[4,2,240]{2,1,0:T(2,128)(2,1)S(1)}, u32[]{:S(2)}, u32[]{:S(2)}) async-start(bf16[4,2,240]{2,1,0:T(2,128)(2,1)} %reshape.466), calls=%async_computation.5 | async-start | bytes 8192 | tf_op jit(solution)/shard_map/all_to_all | solution.py:205
  556.6 6.2 copy-start.13
  556.6 124.9 %all-to-all-start.3 = ((bf16[32,48,2560]{2,1,0:T(8,128)(2,1)}), bf16[32,48,2560]{2,1,0:T(8,128)(2,1)}, u32[]{:S(2)}, u32[]{:S(2)}) async-start(bf16[32,48,2560]{2,1,0:T(8,128)(2,1)} %bitcast.90), calls=%async_computation.3 | async-start | bytes 15728640 | tf_op jit(solution)/shard_map/all_to_all | solution.py:24
Sparse Core Ops, SparseCore 0:
  21.2 75.2 all-gather.2
  273.3 75.0 all-gather.4
  359.5 159.6 reduce-scatter.1
